TPU v7x, 32 devices: a whole 2x2x4 slice. The times are simulated.
32 devices in a mesh: dp: 8 (over z, y), feat: 4 (over x, core).
Axes of the slice: x: 2, y: 2, z: 4, core: 2. Of those that a mesh axis runs over, the one named last changes fastest.
Arguments:
- activations: bfloat16 [16384, 2048], P('feat', 'dp'), may hold values from -6 to 6
- cotangent: bfloat16 [16384, 2048], P('feat', 'dp'), may hold values from -6 to 6
- r_mix: bfloat16 [64, 256, 256], P('feat', 'dp'), may hold values from -0.375 to 0.375
- l_mix: bfloat16 [256, 4096], P('feat', 'dp'), may hold values from -0.75 to 0.75
Outputs:
- grad_x: bfloat16 [16384, 2048], P('feat', 'dp')
- grad_r: float32 [64, 256, 256], P('feat', 'dp')
- grad_l: float32 [256, 4096], P('feat', 'dp')
All inputs are finite; a program needn't handle non-finite values.
Results may differ from a plain program's by a relative error of at most 0.0055.
Values may be sent and summed in bfloat16 or wider, within the bound.
No kernel may reach another device: no remote copies, remote signals or barrier semaphores. Data moves between devices by JAX's collectives and lax.ppermute only.
A program may use at most 64 MiB of HBM per device.

v0:
```python
import math
import jax
import jax.numpy as jnp
from jax import lax
from jax.sharding import PartitionSpec as P

BLOCKS = 64
WIDTH = 256


def gelu_tanh(values):
    return jax.nn.gelu(values, approximate=True)


def slope_of(pre_act, upstream):
    _, pullback = jax.vjp(gelu_tanh, pre_act)
    return pullback(upstream.astype(jnp.float32))[0].astype(jnp.bfloat16)


def body(activations, cotangent, r_mix, l_mix):
    tok_count = activations.shape[1]
    local_blocks = activations.shape[0] // WIDTH
    grad_scale = 1.0 / math.sqrt(tok_count * lax.axis_size("dp"))
    r_whole, l_whole = (
        lax.all_gather(r_mix, "dp", axis=1, tiled=True),
        lax.all_gather(l_mix, "dp", axis=1, tiled=True),
    )
    local_cols = l_whole.shape[0]
    l_blocks = l_whole.reshape(local_cols, BLOCKS, BLOCKS)
    x_blocks = activations.reshape(local_blocks, WIDTH, tok_count)
    g_blocks = cotangent.reshape(local_blocks, WIDTH, tok_count)
    mixed_rows = jnp.einsum(
        "bit,bio->bot", x_blocks, r_whole, preferred_element_type=jnp.float32
    ).astype(jnp.bfloat16)
    outgoing = (mixed_rows,)
    parts = (lax.all_to_all(outgoing[0], "feat", split_axis=1, concat_axis=0, tiled=True),)
    columns = parts[0]
    pre_act = jnp.einsum("bst,sbc->cst", columns, l_blocks, preferred_element_type=jnp.float32)
    arrived = (columns, pre_act) + tuple(parts[1:])
    columns = arrived[0]
    pre_act = arrived[1]
    pre_rows = lax.all_to_all(pre_act, "feat", split_axis=0, concat_axis=1, tiled=True)
    slope_rows = slope_of(pre_rows, g_blocks)
    slope_cols = lax.all_to_all(slope_rows, "feat", split_axis=1, concat_axis=0, tiled=True)
    back_cols = jnp.einsum(
        "cst,sbc->bst", slope_cols, l_blocks, preferred_element_type=jnp.float32
    ).astype(jnp.bfloat16)
    l_term = jnp.einsum("bst,cst->sbc", columns, slope_cols, preferred_element_type=jnp.float32)
    l_term = l_term.reshape(local_cols, BLOCKS * BLOCKS) * grad_scale
    back_rows = lax.all_to_all(back_cols, "feat", split_axis=0, concat_axis=1, tiled=True)
    back_rows, through_r = (
        back_rows,
        jnp.einsum("bot,bio->bit", back_rows, r_whole, preferred_element_type=jnp.float32),
    )
    grad_x = (
        (g_blocks.astype(jnp.float32) + through_r)
        .astype(jnp.bfloat16)
        .reshape(local_blocks * WIDTH, tok_count)
    )
    r_term = (
        jnp.einsum("bit,bot->bio", x_blocks, back_rows, preferred_element_type=jnp.float32)
        * grad_scale
    )
    grad_l, grad_r = (
        lax.psum_scatter(l_term, "dp", scatter_dimension=1, tiled=True),
        lax.psum_scatter(r_term, "dp", scatter_dimension=1, tiled=True),
    )
    return (grad_x, grad_r, grad_l)


def solution(mesh):
    placed = (P("feat", "dp"), P("feat", "dp"), P("feat", "dp", None), P("feat", "dp"))
    return jax.shard_map(
        body,
        mesh=mesh,
        in_specs=placed,
        out_specs=(P("feat", "dp"), P("feat", "dp", None), P("feat", "dp")),
        check_vma=False,
    )
```

profile of v0, /device:TPU:0, one launch (start us, length us, event | category | flops | bytes accessed | tf_op | source)
XLA Modules:
  0.0 399.9 jit_solution(9625601833998472881)
XLA Ops:
  7.9 54.3 %all-gather.2.cloned.1.call-done = bf16[16,256,256]{2,1,0:T(8,128)(2,1)} async-done(((bf16[16,32,256]{2,1,0:T(8,128)(2,1)}), bf16[16,256,256]{2,1,0:T(8,128)(2,1)}) %all-gather.2.cloned.1.call-update) | async-done | bytes 2097168 | tf_op jit(solution)/shard_map/all_gather | solution.py:25
  62.2 2.4 convolution_convert_fusion
  64.6 2.5 copy.19
  67.1 4.6 %all-to-all-start = ((bf16[16,256,256]{2,0,1:T(8,128)(2,1)}), bf16[16,256,256]{2,0,1:T(8,128)(2,1)}, u32[]{:S(2)}, u32[]{:S(2)}) async-start(bf16[16,256,256]{2,0,1:T(8,128)(2,1)} %copy.19), calls=%async_computation | async-start | bytes 4194304 | tf_op jit(solution)/shard_map/all_to_all | solution.py:36
  71.7 33.3 %all_gather.7 = bf16[64,4096]{1,0:T(8,128)(2,1)} all-gather(bf16[64,512]{1,0:T(8,128)(2,1)S(1)} %copy-done.5), channel_id=1, replica_groups=mesh['dp'=8,'feat'=4] {'dp'}, dimensions={1}, use_global_device_ids=true | all-gather | bytes 589824 | tf_op jit(solution)/shard_map/all_gather | solution.py:26
  105.0 2.1 reshape.22
  107.1 1.8 copy.20
  109.0 1.3 copy-done.1
  111.0 2.4 copy.22
  113.5 51.1 %all_to_all.72 = f32[64,64,256]{2,1,0:T(8,128)S(1)} all-to-all(f32[64,64,256]{2,1,0:T(8,128)S(1)} %copy.22), channel_id=1, replica_groups=mesh['dp'=8,'feat'=4] {'feat'}, dimensions={0} | all-to-all | bytes 8388608 | tf_op jit(solution)/shard_map/all_to_all | solution.py:42
  166.1 3.3 fusion.6
  169.5 1.2 copy.24
  170.6 28.2 %all_to_all.73 = bf16[16,256,256]{2,0,1:T(8,128)(2,1)S(1)} all-to-all(bf16[16,256,256]{2,0,1:T(8,128)(2,1)S(1)} %copy.24), channel_id=1, replica_groups=mesh['dp'=8,'feat'=4] {'feat'}, dimensions={1} | all-to-all | bytes 4194304 | tf_op jit(solution)/shard_map/all_to_all | solution.py:44
  200.4 1.2 copy.26
  201.6 28.2 %all_to_all.74 = bf16[64,64,256]{2,1,0:T(8,128)(2,1)S(1)} all-to-all(bf16[64,64,256]{2,1,0:T(8,128)(2,1)S(1)} %copy.26), channel_id=1, replica_groups=mesh['dp'=8,'feat'=4] {'feat'}, dimensions={0} | all-to-all | bytes 4194304 | tf_op jit(solution)/shard_map/all_to_all | solution.py:50
  230.0 1.3 copy-done.3
  231.4 2.7 multiply_bitcast_fusion
  234.1 5.5 %copy.28 = f32[16,256,256]{2,0,1:T(8,128)} copy(f32[16,256,256]{1,2,0:T(8,128)} %multiply_bitcast_fusion) | data formatting | bytes 8388608 | tf_op jit(solution)/shard_map/mul | solution.py:61
  239.6 4.2 %convolution_multiply_fusion = f32[64,64,64]{2,1,0:T(8,128)} fusion(bf16[64,64,256]{2,0,1:T(8,128)(2,1)} %bitcast.50, bf16[64,64,256]{2,0,1:T(8,128)(2,1)} %bitcast.52), kind=kOutput, calls=%fused_computation.20 | convolution fusion | flops 134479872 | bytes 5242880 | tf_op jit(solution)/shard_map/bst,cst->sbc/dot_general | solution.py:48
  243.9 3.1 mul.78
  247.0 4.9 %fusion.10 = bf16[16,256,256]{2,1,0:T(8,128)(2,1)} fusion(bf16[16,256,256]{2,1,0:T(8,128)(2,1)} %bitcast.58, bf16[16,256,256]{2,1,0:T(8,128)(2,1)} %all-gather.2.cloned.1.call-done, bf16[16,256,256]{2,1,0:T(8,128)(2,1)} %bitcast.54), kind=kOutput, calls=%fused_computation.15 | convolution fusion | flops 540016640 | bytes 8388608 | tf_op jit(solution)/shard_map/bot,bio->bit/dot_general | solution.py:53
  251.9 73.5 %reduce-scatter.3.cloned.1.call-done = f32[16,32,256]{2,0,1:T(8,128)} async-done(((f32[16,256,256]{2,0,1:T(8,128)}), f32[16,32,256]{2,0,1:T(8,128)}) %reduce-scatter.3.cloned.1.call-update) | async-done | bytes 524304 | tf_op jit(solution)/shard_map/reduce_scatter | solution.py:66
  325.4 2.1 copy.29
  327.6 65.8 %reduce-scatter.5.cloned.1.call-done = f32[64,512]{1,0:T(8,128)} async-done(((f32[64,4096]{1,0:T(8,128)}), f32[64,512]{1,0:T(8,128)}) %reduce-scatter.5.cloned.1.call-update) | async-done | bytes 131088 | tf_op jit(solution)/shard_map/reduce_scatter | solution.py:65
  (22 shorter events, 5.0 us)
Async XLA Ops:
  7.2 55.0 %copy-start = (bf16[4096,256]{1,0:T(8,128)(2,1)S(1)}, bf16[4096,256]{1,0:T(8,128)(2,1)}, u32[]{:S(2)}) copy-start(bf16[4096,256]{1,0:T(8,128)(2,1)} %param.4) | copy-start | bytes 6291460
  7.2 55.0 %all-gather.2.cloned.1.call-start = ((), (), s32[]{:S(2)}) async-start(), calls=%async_computation.6 | async-start | bytes 2359296 | tf_op jit(solution)/shard_map/all_gather | solution.py:25
  67.1 4.6 %copy-start.5 = (bf16[64,512]{1,0:T(8,128)(2,1)S(1)}, bf16[64,512]{1,0:T(8,128)(2,1)}, u32[]{:S(2)}) copy-start(bf16[64,512]{1,0:T(8,128)(2,1)} %param.7) | copy-start | bytes 196612
  67.1 40.0 %all-to-all-start = ((bf16[16,256,256]{2,0,1:T(8,128)(2,1)}), bf16[16,256,256]{2,0,1:T(8,128)(2,1)}, u32[]{:S(2)}, u32[]{:S(2)}) async-start(bf16[16,256,256]{2,0,1:T(8,128)(2,1)} %copy.19), calls=%async_computation | async-start | bytes 4194304 | tf_op jit(solution)/shard_map/all_to_all | solution.py:36
  71.6 253.8 %reduce-scatter.3.cloned.1.call-start = ((), (), s32[]{:S(2)}) async-start(), calls=%async_computation.7 | async-start | bytes 4718592 | tf_op jit(solution)/shard_map/reduce_scatter | solution.py:66
  109.0 1.3 copy-start.1
  164.6 1.6 copy-start.4
  199.1 1.3 copy-start.2
  230.0 1.3 copy-start.3
  239.6 153.8 %reduce-scatter.5.cloned.1.call-start = ((), (), s32[]{:S(2)}) async-start(), calls=%async_computation.8 | async-start | bytes 1179648 | tf_op jit(solution)/shard_map/reduce_scatter | solution.py:65
Sparse Core Ops, SparseCore 0:
  10.2 51.9 all-gather.1
  239.7 85.6 reduce-scatter.2
  329.8 63.5 reduce-scatter.4
where the time goes:
time: 401 us; the launch traced here: 400 us
  waiting for transfers between devices  194 us (48%)
  blocking collectives  141 us (35%)
  local copies, waits for them, and re-layouts  27.3 us (7%)
  matrix products  15.7 us (4%)
  between operations  13.9 us (3%)
  starting transfers between devices  4.69 us (1%)
    reduce_scatter x1, waiting for transfers between devices, body(): lax.psum_scatter(r_term, 'dp', scatter_dimension=1, tiled=True)  73.5 us
    reduce_scatter x1, waiting for transfers between devices, body(): lax.psum_scatter(l_term, 'dp', scatter_dimension=1, tiled=True)  65.8 us
    all_gather x1, waiting for transfers between devices, body(): lax.all_gather(r_mix, 'dp', axis=1, tiled=True)  54.3 us
    all_to_all x1, blocking collectives, body(): lax.all_to_all(pre_act, 'feat', split_axis=0, concat_axis=1, tiled=True)  51.1 us
    all_gather x1, blocking collectives, body(): lax.all_gather(l_mix, 'dp', axis=1, tiled=True)  33.3 us
    all_to_all x1, blocking collectives, body(): lax.all_to_all(slope_rows, 'feat', split_axis=1, concat_axis=0, tiled=True)  28.2 us
    all_to_all x1, blocking collectives, body(): lax.all_to_all(back_cols, 'feat', split_axis=0, concat_axis=1, tiled=True)  28.2 us
  transfers between devices with their start and end apart: 4, of which 3 were waited for; matrix products, arithmetic and copies ran while one was open for 4% of the time, Pallas kernels for 0%

commit v1 on v0

--- a/solution.py
+++ b/solution.py
@@ -6,6 +6,28 @@
 
 BLOCKS = 64
 WIDTH = 256
+
+
+def cut_along(x, dim, size):
+    before, after = (x.shape[:dim], x.shape[dim + 1 :])
+    return jnp.moveaxis(x.reshape(*before, size, -1, *after), dim, 0)
+
+
+def joined_along(blocks, dim):
+    lengths = list(blocks.shape[1:])
+    lengths[dim] *= blocks.shape[0]
+    return jnp.moveaxis(blocks, 0, dim).reshape(lengths)
+
+
+def swapped_with_each(value, axis, split_dim, concat_dim):
+    count, place = (lax.axis_size(axis), lax.axis_index(axis))
+    pieces = cut_along(value, split_dim, count)
+    done = [pieces[place]]
+    for step in range(1, count):
+        sent = pieces[place ^ step]
+        done.append(lax.ppermute(sent, axis, [(i, i ^ step) for i in range(count)]))
+    pieces = jnp.stack(done)[place ^ jnp.arange(count)]
+    return joined_along(pieces, concat_dim)
 
 
 def gelu_tanh(values):
@@ -39,7 +61,7 @@
     arrived = (columns, pre_act) + tuple(parts[1:])
     columns = arrived[0]
     pre_act = arrived[1]
-    pre_rows = lax.all_to_all(pre_act, "feat", split_axis=0, concat_axis=1, tiled=True)
+    pre_rows = swapped_with_each(pre_act, "feat", 0, 1)
     slope_rows = slope_of(pre_rows, g_blocks)
     slope_cols = lax.all_to_all(slope_rows, "feat", split_axis=1, concat_axis=0, tiled=True)
     back_cols = jnp.einsum(

time: 401 us -> 406 us (1.012)
  blocking collectives: 141 us -> 89.7 us
  waiting for transfers between devices: 194 us -> 240 us
  local copies, waits for them, and re-layouts: 27.3 us -> 32.9 us
    all_to_all x1 -> x0, blocking collectives: 51.1 us -> none  [body(): lax.all_to_all(pre_act, 'feat', split_axis=0, concat_axis=1, tiled=True)]
    ppermute x0 -> x3, waiting for transfers between devices: none -> 46 us  [swapped_with_each(): done.append(lax.ppermute(sent, axis, [(i, i ^ step) for i in range(count)]))]
    gather x0 -> x1, local copies, waits for them, and re-layouts: none -> 4.97 us  [swapped_with_each(): pieces = jnp.stack(done)[place ^ jnp.arange(count)]]
  transfers between devices with their start and end apart: 4 -> 7, of which waited for: 3 -> 5; matrix products, arithmetic and copies ran while one was open for 4% -> 4% of each run, Pallas kernels for 0% -> 0%
where the time goes in v1:
time: 406 us; the launch traced here: 405 us
  waiting for transfers between devices  240 us (59%)
  blocking collectives  89.7 us (22%)
  local copies, waits for them, and re-layouts  32.9 us (8%)
  matrix products  15.7 us (4%)
  between operations  13.9 us (3%)
  starting transfers between devices  6.69 us (2%)
  other arithmetic  5.91 us (1%)
    reduce_scatter x1, waiting for transfers between devices, body(): lax.psum_scatter(r_term, 'dp', scatter_dimension=1, tiled=True)  73.6 us
    reduce_scatter x1, waiting for transfers between devices, body(): lax.psum_scatter(l_term, 'dp', scatter_dimension=1, tiled=True)  65.9 us
    all_gather x1, waiting for transfers between devices, body(): lax.all_gather(r_mix, 'dp', axis=1, tiled=True)  54.3 us
    ppermute x3, waiting for transfers between devices, swapped_with_each(): done.append(lax.ppermute(sent, axis, [(i, i ^ step) for i in range(count)]))  46 us
    all_gather x1, blocking collectives, body(): lax.all_gather(l_mix, 'dp', axis=1, tiled=True)  33.3 us
    all_to_all x1, blocking collectives, body(): lax.all_to_all(slope_rows, 'feat', split_axis=1, concat_axis=0, tiled=True)  28.2 us
    all_to_all x1, blocking collectives, body(): lax.all_to_all(back_cols, 'feat', split_axis=0, concat_axis=1, tiled=True)  28.2 us
  transfers between devices with their start and end apart: 7, of which 5 were waited for; matrix products, arithmetic and copies ran while one was open for 4% of the time, Pallas kernels for 0%

profile of v1, /device:TPU:0, one launch (start us, length us, event | category | flops | bytes accessed | tf_op | source)
XLA Modules:
  0.0 405.2 jit_solution(717810089733160234)
XLA Ops:
  7.9 54.3 %all-gather.2.cloned.1.call-done = bf16[16,256,256]{2,1,0:T(8,128)(2,1)} async-done(((bf16[16,32,256]{2,1,0:T(8,128)(2,1)}), bf16[16,256,256]{2,1,0:T(8,128)(2,1)}) %all-gather.2.cloned.1.call-update) | async-done | bytes 2097168 | tf_op jit(solution)/shard_map/all_gather | solution.py:47
  62.2 2.4 convolution_convert_fusion
  64.6 2.5 copy.19
  67.1 4.6 %all-to-all-start = ((bf16[16,256,256]{2,0,1:T(8,128)(2,1)}), bf16[16,256,256]{2,0,1:T(8,128)(2,1)}, u32[]{:S(2)}, u32[]{:S(2)}) async-start(bf16[16,256,256]{2,0,1:T(8,128)(2,1)} %copy.19), calls=%async_computation | async-start | bytes 4194304 | tf_op jit(solution)/shard_map/all_to_all | solution.py:58
  71.7 33.3 %all_gather.7 = bf16[64,4096]{1,0:T(8,128)(2,1)} all-gather(bf16[64,512]{1,0:T(8,128)(2,1)S(1)} %copy-done.5), channel_id=1, replica_groups=mesh['dp'=8,'feat'=4] {'dp'}, dimensions={1}, use_global_device_ids=true | all-gather | bytes 589824 | tf_op jit(solution)/shard_map/all_gather | solution.py:48
  105.0 2.1 reshape.44
  107.1 1.8 copy.20
  111.0 1.9 collective-permute-start.1
  112.9 23.2 %collective-permute-done.2 = f32[16,64,256]{2,0,1:T(8,128)S(1)} collective-permute-done((f32[16,64,256]{2,0,1:T(8,128)S(1)}, f32[16,64,256]{2,0,1:T(8,128)S(1)}, u32[]{:S(2)}, u32[]{:S(2)}) %collective-permute-start.2) | collective-permute-done | bytes 1048608 | tf_op jit(solution)/shard_map/ppermute | solution.py:28
  136.1 22.8 %collective-permute-done.1 = f32[16,64,256]{2,0,1:T(8,128)S(1)} collective-permute-done((f32[16,64,256]{2,0,1:T(8,128)S(1)}, f32[16,64,256]{2,0,1:T(8,128)S(1)}, u32[]{:S(2)}, u32[]{:S(2)}) %collective-permute-start.1) | collective-permute-done | bytes 1048608 | tf_op jit(solution)/shard_map/ppermute | solution.py:28
  158.9 2.6 pad_maximum_fusion
  161.5 5.0 %gather_fusion = f32[4,16,64,256]{3,1,2,0:T(8,128)} fusion(f32[4,16,64,256]{3,1,0,2:T(8,128)} %pad_maximum_fusion, s32[1024]{0:T(1024)S(1)} %pad_clamp_fusion), kind=kCustom, calls=%fused_computation | custom fusion | bytes 8388624 | tf_op jit(solution)/shard_map/gather | solution.py:29
  166.4 4.8 %copy.22 = f32[16,4,64,256]{3,2,1,0:T(8,128)S(1)} copy(f32[16,4,64,256]{3,0,2,1:T(8,128)} %bitcast.66) | data formatting | bytes 8388608 | tf_op jit(solution)/shard_map/transpose | solution.py:19
  171.2 3.3 fusion.6
  175.7 28.2 %all_to_all.54 = bf16[16,256,256]{2,0,1:T(8,128)(2,1)S(1)} all-to-all(bf16[16,256,256]{2,0,1:T(8,128)(2,1)S(1)} %copy.23), channel_id=1, replica_groups=mesh['dp'=8,'feat'=4] {'feat'}, dimensions={1} | all-to-all | bytes 4194304 | tf_op jit(solution)/shard_map/all_to_all | solution.py:66
  206.7 28.2 %all_to_all.55 = bf16[64,64,256]{2,1,0:T(8,128)(2,1)S(1)} all-to-all(bf16[64,64,256]{2,1,0:T(8,128)(2,1)S(1)} %copy.25), channel_id=1, replica_groups=mesh['dp'=8,'feat'=4] {'feat'}, dimensions={0} | all-to-all | bytes 4194304 | tf_op jit(solution)/shard_map/all_to_all | solution.py:72
  236.5 2.7 multiply_bitcast_fusion
  239.2 5.5 %copy.27 = f32[16,256,256]{2,0,1:T(8,128)} copy(f32[16,256,256]{1,2,0:T(8,128)} %multiply_bitcast_fusion) | data formatting | bytes 8388608 | tf_op jit(solution)/shard_map/mul | solution.py:83
  244.8 4.3 %convolution_multiply_fusion = f32[64,64,64]{2,1,0:T(8,128)} fusion(bf16[64,64,256]{2,0,1:T(8,128)(2,1)} %bitcast.60, bf16[64,64,256]{2,0,1:T(8,128)(2,1)} %bitcast.62), kind=kOutput, calls=%fused_computation.21 | convolution fusion | flops 134479872 | bytes 5242880 | tf_op jit(solution)/shard_map/bst,cst->sbc/dot_general | solution.py:70
  249.0 3.2 mul.78
  252.2 4.9 %fusion.10 = bf16[16,256,256]{2,1,0:T(8,128)(2,1)} fusion(bf16[16,256,256]{2,1,0:T(8,128)(2,1)} %bitcast.69, bf16[16,256,256]{2,1,0:T(8,128)(2,1)} %all-gather.2.cloned.1.call-done, bf16[16,256,256]{2,1,0:T(8,128)(2,1)} %bitcast.64), kind=kOutput, calls=%fused_computation.16 | convolution fusion | flops 540016640 | bytes 8388608 | tf_op jit(solution)/shard_map/bot,bio->bit/dot_general | solution.py:75
  257.1 73.6 %reduce-scatter.3.cloned.1.call-done = f32[16,32,256]{2,0,1:T(8,128)} async-done(((f32[16,256,256]{2,0,1:T(8,128)}), f32[16,32,256]{2,0,1:T(8,128)}) %reduce-scatter.3.cloned.1.call-update) | async-done | bytes 524304 | tf_op jit(solution)/shard_map/reduce_scatter | solution.py:88
  330.7 2.1 copy.28
  332.9 65.9 %reduce-scatter.5.cloned.1.call-done = f32[64,512]{1,0:T(8,128)} async-done(((f32[64,4096]{1,0:T(8,128)}), f32[64,512]{1,0:T(8,128)}) %reduce-scatter.5.cloned.1.call-update) | async-done | bytes 131088 | tf_op jit(solution)/shard_map/reduce_scatter | solution.py:87
  (31 shorter events, 8.4 us)
Async XLA Ops:
  7.2 55.0 %copy-start = (bf16[4096,256]{1,0:T(8,128)(2,1)S(1)}, bf16[4096,256]{1,0:T(8,128)(2,1)}, u32[]{:S(2)}) copy-start(bf16[4096,256]{1,0:T(8,128)(2,1)} %param.4) | copy-start | bytes 6291460
  7.2 55.0 %all-gather.2.cloned.1.call-start = ((), (), s32[]{:S(2)}) async-start(), calls=%async_computation.5 | async-start | bytes 2359296 | tf_op jit(solution)/shard_map/all_gather | solution.py:47
  67.1 4.7 %copy-start.5 = (bf16[64,512]{1,0:T(8,128)(2,1)S(1)}, bf16[64,512]{1,0:T(8,128)(2,1)}, u32[]{:S(2)}) copy-start(bf16[64,512]{1,0:T(8,128)(2,1)} %param.7) | copy-start | bytes 196612
  67.1 40.1 %all-to-all-start = ((bf16[16,256,256]{2,0,1:T(8,128)(2,1)}), bf16[16,256,256]{2,0,1:T(8,128)(2,1)}, u32[]{:S(2)}, u32[]{:S(2)}) async-start(bf16[16,256,256]{2,0,1:T(8,128)(2,1)} %copy.19), calls=%async_computation | async-start | bytes 4194304 | tf_op jit(solution)/shard_map/all_to_all | solution.py:58
  71.6 259.1 %reduce-scatter.3.cloned.1.call-start = ((), (), s32[]{:S(2)}) async-start(), calls=%async_computation.6 | async-start | bytes 4718592 | tf_op jit(solution)/shard_map/reduce_scatter | solution.py:88
  109.0 1.3 copy-start.1
  110.9 25.2 %collective-permute-start.2 = (f32[16,64,256]{2,0,1:T(8,128)S(1)}, f32[16,64,256]{2,0,1:T(8,128)S(1)}, u32[]{:S(2)}, u32[]{:S(2)}) collective-permute-start(f32[16,64,256]{2,0,1:T(8,128)S(1)} %get-tuple-element.13), channel_id=1, source_target_pairs={{0,3},{1,2},{2,1},{3,0},{4,7},{5,6},{6,5},{7,4},{8,11},{9,10},{10,... | collective-permute-start | bytes 3145736 | tf_op jit(solution)/shard_map/ppermute | solution.py:28
  111.0 47.9 %collective-permute-start.1 = (f32[16,64,256]{2,0,1:T(8,128)S(1)}, f32[16,64,256]{2,0,1:T(8,128)S(1)}, u32[]{:S(2)}, u32[]{:S(2)}) collective-permute-start(f32[16,64,256]{2,0,1:T(8,128)S(1)} %get-tuple-element.14), channel_id=1, source_target_pairs={{0,2},{1,3},{2,0},{3,1},{4,6},{5,7},{6,4},{7,5},{8,10},{9,11},{10,... | collective-permute-start | bytes 3145736 | tf_op jit(solution)/shard_map/ppermute | solution.py:28
  112.9 46.0 %collective-permute-start = (f32[16,64,256]{2,0,1:T(8,128)S(1)}, f32[16,64,256]{2,0,1:T(8,128)S(1)}, u32[]{:S(2)}, u32[]{:S(2)}) collective-permute-start(f32[16,64,256]{2,0,1:T(8,128)S(1)} %get-tuple-element.15), channel_id=1, source_target_pairs={{0,1},{1,0},{2,3},{3,2},{4,5},{5,4},{6,7},{7,6},{8,9},{9,8},{10,11... | collective-permute-start | bytes 3145736 | tf_op jit(solution)/shard_map/ppermute | solution.py:28
  166.4 4.8 %copy-start.4 = (bf16[4096,256]{1,0:T(8,128)(2,1)S(1)}, bf16[4096,256]{1,0:T(8,128)(2,1)}, u32[]{:S(2)}) copy-start(bf16[4096,256]{1,0:T(8,128)(2,1)} %param.5) | copy-start | bytes 6291460
  204.2 1.3 copy-start.2
  235.1 1.3 copy-start.3
  244.7 154.0 %reduce-scatter.5.cloned.1.call-start = ((), (), s32[]{:S(2)}) async-start(), calls=%async_computation.7 | async-start | bytes 1179648 | tf_op jit(solution)/shard_map/reduce_scatter | solution.py:87
Sparse Core Ops, SparseCore 0:
  10.2 51.9 all-gather.1
  244.8 85.8 reduce-scatter.2
  335.1 63.5 reduce-scatter.4
